TPU v7x, 256 devices: a whole 4x4x8 slice. The times are simulated.
256 devices in a mesh: det: 16 (over z, core), orb: 16 (over x, y).
Axes of the slice: x: 4, y: 4, z: 8, core: 2. Of those that a mesh axis runs over, the one named last changes fastest.
Arguments:
- orbitals: bfloat16 [64, 1024, 256], P('det', 'orb'), may hold values from -0.06 to 1.06
- dfit: bfloat16 [64, 1024, 1024], P('orb'), may hold values from -0.5 to 0.5, as said below
- pair_left: int32 [32], P('det'), may hold values from 0 to 63, as said below
- pair_right: int32 [32], P('det'), may hold values from 0 to 63
- pair_count: int32 [16], P('det'), may hold values from 1 to 2, as said below
- pair_weight: float32 [32], P('det'), may hold values from 1 to 4
- aux_screen: int32 [32, 64], P('det', 'orb'), may hold values 0 or 1
Outputs:
- gradient: float32 [64, 1024, 256], P('det', 'orb')
Inputs may be any that keep to these rules, and one draw needn't show every extreme that they name: `pair_left`: slot s names a determinant among numbers (s // 2) * 4 to (s // 2 + 1) * 4 - 1. `pair_count`: some det index has all 2 slots live. `dfit`: every matrix is symmetric.
All inputs are finite; a program needn't handle non-finite values. No bound on the sum of `aux_screen` on one device may be relied on, other than what follows from the above.
Results may differ from a plain program's by a relative error of at most 0.0022.
Values may be sent and summed in bfloat16 or wider, within the bound.
No kernel may reach another device: no remote copies, remote signals or barrier semaphores. Data moves between devices by JAX's collectives and lax.ppermute only.
A program may use at most 64 MiB of HBM per device.

v0:
```python
import jax
import jax.numpy as jnp
from jax import lax
from jax.sharding import PartitionSpec as P

NS = 3


def newton(correlation):
    eye = jnp.eye(correlation.shape[-1], dtype=jnp.float32)
    inverse = jnp.broadcast_to(eye, correlation.shape)
    for sweep in range(NS):
        product = jnp.einsum("bij,bjk->bik", correlation, inverse, precision=lax.Precision.HIGHEST)
        inverse = jnp.einsum(
            "bij,bjk->bik", inverse, 2.0 * eye - product, precision=lax.Precision.HIGHEST
        )
    return inverse


def process(dfit, left_rows, right_rows, weights, screen):
    correlation_part = jnp.einsum(
        "brc,brd->bcd", left_rows, right_rows, preferred_element_type=jnp.float32
    )
    correlation = lax.psum(correlation_part, "orb")
    inverse = newton(correlation)
    moved_rows = jnp.einsum(
        "brc,bcd->brd", right_rows.astype(jnp.float32), inverse, precision=lax.Precision.HIGHEST
    ).astype(jnp.bfloat16)
    left_full, moved_full = (
        lax.all_gather(left_rows, "orb", axis=1, tiled=True),
        lax.all_gather(moved_rows, "orb", axis=1, tiled=True),
    )
    applied = jnp.einsum(
        "qst,btc->bqsc", dfit, moved_full, preferred_element_type=jnp.float32
    ).astype(jnp.bfloat16)
    projected = jnp.einsum(
        "bsc,qst->bqct", left_full, dfit, preferred_element_type=jnp.float32
    ).astype(jnp.bfloat16)
    exchange = jnp.einsum(
        "bqct,btd->bqcd", projected, moved_full, preferred_element_type=jnp.float32
    )
    factor = 2.0 * weights[:, None, None, None] * screen.astype(jnp.float32)[:, :, None, None]
    scaled = (factor * exchange).astype(jnp.bfloat16)
    left_term = jnp.einsum("bqsc,bqdc->sbd", applied, scaled, preferred_element_type=jnp.float32)
    moved_term = jnp.einsum("bqcs,bqcd->sbd", projected, scaled, preferred_element_type=jnp.float32)
    summed = lax.psum_scatter(
        jnp.concatenate([left_term, moved_term], axis=1), "orb", scatter_dimension=0, tiled=True
    )
    batch = left_rows.shape[0]
    left_grad = jnp.transpose(summed[:, :batch], (1, 0, 2))
    moved_grad = jnp.transpose(summed[:, batch:], (1, 0, 2))
    right_grad = jnp.einsum("brc,bdc->brd", moved_grad, inverse, precision=lax.Precision.HIGHEST)
    return (left_grad, right_grad)


def local(orbitals, dfit, pair_left, pair_right, pair_count, pair_weight, aux_screen):
    det_local = orbitals.shape[0]
    capacity = pair_left.shape[0]
    slot_index = jnp.arange(capacity, dtype=jnp.int32)
    weights = jnp.where(slot_index < pair_count[0], pair_weight, jnp.zeros_like(pair_weight))
    left_local = pair_left % det_local
    left_rows = jnp.take(orbitals, left_local, axis=0)
    everyone = lax.all_gather(orbitals, "det", axis=0, tiled=True)
    right_rows = jnp.take(everyone, pair_right, axis=0)

    def one_slot(slot, grads):

        def select_slot(array):
            return lax.dynamic_slice_in_dim(array, slot, 1, 0)

        left_one, right_one = process(
            dfit,
            select_slot(left_rows),
            select_slot(right_rows),
            select_slot(weights),
            select_slot(aux_screen),
        )
        return (
            lax.dynamic_update_slice_in_dim(grads[0], left_one, slot, 0),
            lax.dynamic_update_slice_in_dim(grads[1], right_one, slot, 0),
        )

    zeros = jnp.zeros(left_rows.shape, jnp.float32)
    left_grad, right_grad = lax.fori_loop(0, capacity, one_slot, (zeros, zeros))
    owners = (left_local[:, None] == jnp.arange(det_local, dtype=jnp.int32)[None, :]).astype(
        jnp.float32
    )
    own_sum = jnp.einsum("pn,prc->nrc", owners, left_grad, precision=lax.Precision.HIGHEST)
    places = jnp.arange(det_local * lax.axis_size("det"), dtype=jnp.int32)
    match = (pair_right[:, None] == places[None, :]).astype(jnp.float32)
    returned = lax.psum_scatter(
        jnp.einsum("pn,prc->nrc", match, right_grad, precision=lax.Precision.HIGHEST),
        "det",
        scatter_dimension=0,
        tiled=True,
    )
    return own_sum + returned


def solution(mesh):
    in_specs = (
        P("det", "orb", None),
        P("orb", None, None),
        P("det"),
        P("det"),
        P("det"),
        P("det"),
        P("det", "orb"),
    )
    out_specs = P("det", "orb", None)
    return jax.shard_map(local, mesh=mesh, in_specs=in_specs, out_specs=out_specs, check_vma=False)
```

profile of v0, /device:TPU:4, one launch (start us, length us, event | category | flops | bytes accessed | tf_op | source)
XLA Modules:
  0.0 620.7 jit_solution(5396601231880543745)
XLA Ops:
  8.6 1.5 gather_fusion
  12.1 39.4 %all-gather.5.cloned.1.call-done = bf16[64,64,256]{2,1,0:T(8,128)(2,1)} async-done(((bf16[4,64,256]{2,1,0:T(8,128)(2,1)}), bf16[64,64,256]{2,1,0:T(8,128)(2,1)}) %all-gather.5.cloned.1.call-update) | async-done | bytes 2097168 | tf_op jit(solution)/shard_map/all_gather | solution.py:63
  51.6 2.1 gather_fusion.1
  53.8 486.6 %while.15 = (s32[]{:T(128)}, f32[2,64,256]{2,0,1:T(2,128)}, f32[2,64,256]{2,0,1:T(2,128)}, f32[2]{0:T(128)S(1)}, s32[2,4]{1,0:T(2,128)}, /*index=5*/bf16[2,64,25...) while((s32[]{:T(128)}, f32[2,64,256]{2,0,1:T(2,128)}, ...), condition=%wide.region_3.4_spmd, body=%wide.region_0.3_spmd.sunk | while | flops 7227064320 | bytes 65279744 | solution.py:84
  54.9 23.7 %all_gather.19 = bf16[1,1024,256]{2,1,0:T(8,128)(2,1)S(1)} all-gather(bf16[1,64,256]{2,1,0:T(8,128)(2,1)S(1)} %constant_dynamic-slice_fusion.6), channel_id=1, replica_groups=mesh['det'=16,'orb'=16] {'orb'}, dimensions={1}, use_global_device_ids=true | all-gather | bytes 557056 | tf_op jit(solution)/shard_map/while/body/eval_jaxpr/all_gather | solution.py:30
  78.5 5.8 convolution_convert_fusion.4
  85.6 64.8 %all-reduce.6.cloned.1.call-done = f32[256,256]{1,0:T(8,128)} async-done(((f32[256,256]{1,0:T(8,128)}), f32[256,256]{1,0:T(8,128)}) %all-reduce.6.cloned.1.call-update) | async-done | bytes 262160 | tf_op jit(solution)/shard_map/while/body/eval_jaxpr/psum | solution.py:24
  154.7 22.7 %all-gather.2 = bf16[1024,256]{1,0:T(8,128)(2,1)S(1)} all-gather(bf16[64,256]{1,0:T(8,128)(2,1)S(1)} %convolution_convert_fusion.5), channel_id=2, replica_groups=mesh['det'=16,'orb'=16] {'orb'}, dimensions={0}, use_global_device_ids=true | all-gather | bytes 557056 | tf_op jit(solution)/shard_map/while/body/eval_jaxpr/all_gather | solution.py:31
  180.5 7.7 %fusion.137 = f32[1024,1,256]{0,2,1:T(8,128)} fusion(bf16[4,256,256]{2,1,0:T(8,128)(2,1)} %copy-done.1, bf16[4,1024,1024]{2,1,0:T(8,128)(2,1)} %get-tuple-element.280, bf16[1024,256]{1,0:T(8,128)(2,1)} %copy-done.2), kind=kOutput, calls=%fused_computation.12.clone.1 | convolution fusion | flops 2685403136 | bytes 10485760 | tf_op jit(solution)/shard_map/while/body/eval_jaxpr/bqsc,bqdc->sbd/dot_general | solution.py:44
  188.2 1.4 pad_maximum_fusion.2
  189.6 2.4 copy.46
  193.8 98.1 %all-reduce.8.cloned.1.call-done = f32[1024,2,256]{2,1,0:T(2,128)} async-done(((f32[1024,2,256]{2,1,0:T(2,128)}), f32[1024,2,256]{2,1,0:T(2,128)}) %all-reduce.8.cloned.1.call-update) | async-done | bytes 2097168 | tf_op jit(solution)/shard_map/while
  297.0 23.4 %all_gather.19 = bf16[1,1024,256]{2,1,0:T(8,128)(2,1)S(1)} all-gather(bf16[1,64,256]{2,1,0:T(8,128)(2,1)S(1)} %constant_dynamic-slice_fusion.6), channel_id=1, replica_groups=mesh['det'=16,'orb'=16] {'orb'}, dimensions={1}, use_global_device_ids=true | all-gather | bytes 557056 | tf_op jit(solution)/shard_map/while/body/eval_jaxpr/all_gather | solution.py:30
  320.4 5.8 convolution_convert_fusion.4
  327.4 67.3 %all-reduce.6.cloned.1.call-done = f32[256,256]{1,0:T(8,128)} async-done(((f32[256,256]{1,0:T(8,128)}), f32[256,256]{1,0:T(8,128)}) %all-reduce.6.cloned.1.call-update) | async-done | bytes 262160 | tf_op jit(solution)/shard_map/while/body/eval_jaxpr/psum | solution.py:24
  399.1 22.7 %all-gather.2 = bf16[1024,256]{1,0:T(8,128)(2,1)S(1)} all-gather(bf16[64,256]{1,0:T(8,128)(2,1)S(1)} %convolution_convert_fusion.5), channel_id=2, replica_groups=mesh['det'=16,'orb'=16] {'orb'}, dimensions={0}, use_global_device_ids=true | all-gather | bytes 557056 | tf_op jit(solution)/shard_map/while/body/eval_jaxpr/all_gather | solution.py:31
  424.9 7.7 %fusion.137 = f32[1024,1,256]{0,2,1:T(8,128)} fusion(bf16[4,256,256]{2,1,0:T(8,128)(2,1)} %copy-done.1, bf16[4,1024,1024]{2,1,0:T(8,128)(2,1)} %get-tuple-element.280, bf16[1024,256]{1,0:T(8,128)(2,1)} %copy-done.2), kind=kOutput, calls=%fused_computation.12.clone.1 | convolution fusion | flops 2685403136 | bytes 10485760 | tf_op jit(solution)/shard_map/while/body/eval_jaxpr/bqsc,bqdc->sbd/dot_general | solution.py:44
  432.5 1.4 pad_maximum_fusion.2
  433.9 2.4 copy.46
  438.2 98.1 %all-reduce.8.cloned.1.call-done = f32[1024,2,256]{2,1,0:T(2,128)} async-done(((f32[1024,2,256]{2,1,0:T(2,128)}), f32[1024,2,256]{2,1,0:T(2,128)}) %all-reduce.8.cloned.1.call-update) | async-done | bytes 2097168 | tf_op jit(solution)/shard_map/while
  540.4 2.8 fusion.39
  543.2 4.4 copy.30
  549.0 63.2 %reduce-scatter.2.cloned.1.call-done = f32[4,64,256]{2,1,0:T(8,128)} async-done(((f32[64,64,256]{2,1,0:T(8,128)}), f32[4,64,256]{2,1,0:T(8,128)}) %reduce-scatter.2.cloned.1.call-update) | async-done | bytes 262160 | tf_op jit(solution)/shard_map/reduce_scatter | solution.py:91
  612.2 1.7 copy_add_fusion
  (102 shorter events, 33.4 us)
Async XLA Ops:
  6.5 45.0 %all-gather.5.cloned.1.call-start = ((), (), s32[]{:S(2)}) async-start(), calls=%async_computation.1 | async-start | bytes 2228224 | tf_op jit(solution)/shard_map/all_gather | solution.py:63
  53.8 486.6 %copy-start.9 = (s32[2]{0:T(128)S(1)}, s32[2]{0:T(128)}, u32[]{:S(2)}) copy-start(s32[2]{0:T(128)} %param.12) | copy-start | bytes 28
  53.8 96.5 %all-reduce.6.cloned.1.call-start = ((), (), s32[]{:S(2)}) async-start(), calls=%async_computation.3 | async-start | bytes 524288 | tf_op jit(solution)/shard_map/while/body/eval_jaxpr/psum | solution.py:24
  54.8 237.1 %all-reduce.8.cloned.1.call-start = ((), (), s32[]{:S(2)}) async-start(), calls=%async_computation.4 | async-start | bytes 4194304 | tf_op jit(solution)/shard_map/while
  78.5 7.0 %copy-start.8 = (s32[2,4]{1,0:T(2,128)S(1)}, s32[2,4]{1,0:T(2,128)}, u32[]{:S(2)}) copy-start(s32[2,4]{1,0:T(2,128)} %get-tuple-element.278) | copy-start | bytes 100 | tf_op jit(solution)/shard_map/while
  150.4 3.3 copy-start
  177.4 0.8 copy-start.2
  179.0 0.8 copy-start.1
  191.9 0.7 copy-start.10
  192.0 101.5 %copy-start.5 = (f32[2,64,256]{2,0,1:T(2,128)S(1)}, f32[2,64,256]{2,0,1:T(2,128)}, u32[]{:S(2)}) copy-start(f32[2,64,256]{2,0,1:T(2,128)} %get-tuple-element.260) | copy-start | bytes 393220 | tf_op jit(solution)/shard_map/while
  192.0 102.5 %copy-start.3 = (f32[2,64,256]{2,0,1:T(2,128)S(1)}, f32[2,64,256]{2,0,1:T(2,128)}, u32[]{:S(2)}) copy-start(f32[2,64,256]{2,0,1:T(2,128)} %get-tuple-element.261) | copy-start | bytes 393220 | tf_op jit(solution)/shard_map/while
  294.4 1.0 copy-start.6
  296.0 98.7 %all-reduce.6.cloned.1.call-start = ((), (), s32[]{:S(2)}) async-start(), calls=%async_computation.3 | async-start | bytes 524288 | tf_op jit(solution)/shard_map/while/body/eval_jaxpr/psum | solution.py:24
  296.9 239.4 %all-reduce.8.cloned.1.call-start = ((), (), s32[]{:S(2)}) async-start(), calls=%async_computation.4 | async-start | bytes 4194304 | tf_op jit(solution)/shard_map/while
  320.4 7.0 %copy-start.8 = (s32[2,4]{1,0:T(2,128)S(1)}, s32[2,4]{1,0:T(2,128)}, u32[]{:S(2)}) copy-start(s32[2,4]{1,0:T(2,128)} %get-tuple-element.278) | copy-start | bytes 100 | tf_op jit(solution)/shard_map/while
  394.7 3.3 copy-start
  421.8 0.8 copy-start.2
  423.3 0.8 copy-start.1
  436.3 0.7 copy-start.10
  436.3 101.5 %copy-start.5 = (f32[2,64,256]{2,0,1:T(2,128)S(1)}, f32[2,64,256]{2,0,1:T(2,128)}, u32[]{:S(2)}) copy-start(f32[2,64,256]{2,0,1:T(2,128)} %get-tuple-element.260) | copy-start | bytes 393220 | tf_op jit(solution)/shard_map/while
  436.3 102.5 %copy-start.3 = (f32[2,64,256]{2,0,1:T(2,128)S(1)}, f32[2,64,256]{2,0,1:T(2,128)}, u32[]{:S(2)}) copy-start(f32[2,64,256]{2,0,1:T(2,128)} %get-tuple-element.261) | copy-start | bytes 393220 | tf_op jit(solution)/shard_map/while
  538.8 1.0 copy-start.6
  540.4 71.8 %reduce-scatter.2.cloned.1.call-start = ((), (), s32[]{:S(2)}) async-start(), calls=%async_computation.2 | async-start | bytes 4456448 | tf_op jit(solution)/shard_map/reduce_scatter | solution.py:91
  547.6 0.9 copy-start.7
  (2 other events, 1.3 us)
Sparse Core Ops, SparseCore 0:
  9.2 42.3 all-gather.4
  57.8 92.5 all-reduce.5
  192.1 99.8 all-reduce.7
  299.7 94.9 all-reduce.5
  436.4 99.8 all-reduce.7
  547.7 64.3 reduce-scatter.1
where the time goes:
time: 621 us
  waiting for transfers between devices  432 us (70%)
  blocking collectives  92.5 us (15%)
  matrix products  44.2 us (7%)
  local copies, waits for them, and re-layouts  27.8 us (4%)
  between operations  14.1 us (2%)
  other arithmetic  7.37 us (1%)
    while x6, waiting for transfers between devices  196 us
    psum x2, waiting for transfers between devices, process(): correlation = lax.psum(correlation_part, 'orb')  132 us
    reduce_scatter x1, waiting for transfers between devices, local(): lax.psum_scatter(jnp.einsum('pn,prc->nrc', match, right_grad, precision=l...  63.2 us
    all_gather x2, blocking collectives, process(): lax.all_gather(left_rows, 'orb', axis=1, tiled=True)  47 us
    all_gather x2, blocking collectives, process(): lax.all_gather(moved_rows, 'orb', axis=1, tiled=True)  45.4 us
    all_gather x1, waiting for transfers between devices, local(): everyone = lax.all_gather(orbitals, 'det', axis=0, tiled=True)  39.4 us
    dot_general x2, matrix products, process(): jnp.einsum('bqsc,bqdc->sbd', applied, scaled, preferred_element_type=jnp....  15.3 us
  transfers between devices with their start and end apart: 6, of which 6 were waited for; matrix products, arithmetic and copies ran while one was open for 3% of the time, Pallas kernels for 0%

commit v1 on v0

--- a/solution.py
+++ b/solution.py
@@ -21,7 +21,11 @@
     correlation_part = jnp.einsum(
         "brc,brd->bcd", left_rows, right_rows, preferred_element_type=jnp.float32
     )
-    correlation = lax.psum(correlation_part, "orb")
+    correlation = correlation_part
+    for hop in (1, 2, 4, 8):
+        correlation = correlation + lax.ppermute(
+            correlation, "orb", [(dev, dev ^ hop) for dev in range(16)]
+        )
     inverse = newton(correlation)
     moved_rows = jnp.einsum(
         "brc,bcd->brd", right_rows.astype(jnp.float32), inverse, precision=lax.Precision.HIGHEST

time: 621 us -> 517 us (0.83)
  waiting for transfers between devices: 432 us -> 321 us
  starting transfers between devices: 0.14 us -> 15.4 us
    psum x2 -> x0, waiting for transfers between devices: 132 us -> none  [process(): correlation = lax.psum(correlation_part, 'orb')]
    ppermute x0 -> x8, waiting for transfers between devices: none -> 24 us  [process(): lax.ppermute(correlation, 'orb', [(dev, dev ^ hop) for dev in range(16)])]
    ppermute x0 -> x8, starting transfers between devices: none -> 15.4 us  [process(): lax.ppermute(correlation, 'orb', [(dev, dev ^ hop) for dev in range(16)])]
    while x6 -> x4, waiting for transfers between devices: 196 us -> 193 us
  transfers between devices with their start and end apart: 6 -> 12, of which waited for: 6 -> 8; matrix products, arithmetic and copies ran while one was open for 3% -> 4% of each run, Pallas kernels for 0% -> 0%
where the time goes in v1:
time: 517 us; the launch traced here: 516 us
  waiting for transfers between devices  321 us (62%)
  blocking collectives  91.7 us (18%)
  matrix products  38.2 us (7%)
  local copies, waits for them, and re-layouts  26.2 us (5%)
  starting transfers between devices  15.4 us (3%)
  between operations  13.8 us (3%)
  other arithmetic  7.58 us (1%)
    while x4, waiting for transfers between devices  193 us
    reduce_scatter x1, waiting for transfers between devices, local(): lax.psum_scatter(jnp.einsum('pn,prc->nrc', match, right_grad, precision=l...  63.2 us
    all_gather x2, blocking collectives, process(): lax.all_gather(left_rows, 'orb', axis=1, tiled=True)  46.3 us
    all_gather x2, blocking collectives, process(): lax.all_gather(moved_rows, 'orb', axis=1, tiled=True)  45.4 us
    all_gather x1, waiting for transfers between devices, local(): everyone = lax.all_gather(orbitals, 'det', axis=0, tiled=True)  39.4 us
    ppermute x8, waiting for transfers between devices, process(): lax.ppermute(correlation, 'orb', [(dev, dev ^ hop) for dev in range(16)])  24 us
    ppermute x8, starting transfers between devices, process(): lax.ppermute(correlation, 'orb', [(dev, dev ^ hop) for dev in range(16)])  15.4 us
    dot_general x2, matrix products, process(): jnp.einsum('bqsc,bqdc->sbd', applied, scaled, preferred_element_type=jnp....  14.6 us
  transfers between devices with their start and end apart: 12, of which 8 were waited for; matrix products, arithmetic and copies ran while one was open for 4% of the time, Pallas kernels for 0%

profile of v1, /device:TPU:4, one launch (start us, length us, event | category | flops | bytes accessed | tf_op | source)
XLA Modules:
  0.0 516.4 jit_solution(10603821030258585320)
XLA Ops:
  12.1 39.4 %all-gather.5.cloned.1.call-done = bf16[64,64,256]{2,1,0:T(8,128)(2,1)} async-done(((bf16[4,64,256]{2,1,0:T(8,128)(2,1)}), bf16[64,64,256]{2,1,0:T(8,128)(2,1)}) %all-gather.5.cloned.1.call-update) | async-done | bytes 2097168 | tf_op jit(solution)/shard_map/all_gather | solution.py:67
  53.8 382.5 %while.15 = (s32[]{:T(128)}, f32[2,64,256]{2,0,1:T(2,128)}, f32[2,64,256]{2,0,1:T(2,128)}, f32[2]{0:T(128)S(1)}, s32[2,4]{1,0:T(2,128)}, /*index=5*/bf16[2,64,25...) while((s32[]{:T(128)}, f32[2,64,256]{2,0,1:T(2,128)}, ...), condition=%wide.region_2.3_spmd, body=%wide.region_0.2_spmd.sunk | while | flops 7227392000 | bytes 64755436 | solution.py:88
  55.6 6.9 %collective-permute-done = f32[1,256,256]{2,1,0:T(8,128)S(1)} collective-permute-done((f32[1,256,256]{2,1,0:T(8,128)S(1)}, f32[1,256,256]{2,1,0:T(8,128)S(1)}, u32[]{:S(2)}, u32[]{:S(2)}) %collective-permute-start) | collective-permute-done | bytes 262176 | tf_op jit(solution)/shard_map/while/body/eval_jaxpr/ppermute | solution.py:26
  62.6 3.1 collective-permute-start.1
  65.7 6.1 %collective-permute-done.1 = f32[1,256,256]{2,1,0:T(8,128)S(1)} collective-permute-done((f32[1,256,256]{2,1,0:T(8,128)S(1)}, f32[1,256,256]{2,1,0:T(8,128)S(1)}, u32[]{:S(2)}, u32[]{:S(2)}) %collective-permute-start.1) | collective-permute-done | bytes 262176 | tf_op jit(solution)/shard_map/while/body/eval_jaxpr/ppermute | solution.py:26
  73.1 23.7 %all_gather.19 = bf16[1,1024,256]{2,1,0:T(8,128)(2,1)S(1)} all-gather(bf16[1,64,256]{2,1,0:T(8,128)(2,1)S(1)} %constant_dynamic-slice_fusion.6), channel_id=1, replica_groups=mesh['det'=16,'orb'=16] {'orb'}, dimensions={1}, use_global_device_ids=true | all-gather | bytes 557056 | tf_op jit(solution)/shard_map/while/body/eval_jaxpr/all_gather | solution.py:34
  98.4 5.8 %convolution_convert_fusion.4 = bf16[256,4,1024]{2,0,1:T(8,128)(2,1)S(1)} fusion(bf16[4,1024,1024]{2,1,0:T(8,128)(2,1)} %get-tuple-element.280, bf16[1,1024,256]{2,1,0:T(8,128)(2,1)S(1)} %all_gather.19), kind=kOutput, calls=%fused_computation.10.clone.1 | convolution fusion | flops 2148532224 | bytes 11010048 | tf_op jit(solution)/shard_map/while/body/eval_jaxpr/bsc,qst->bqct/dot_general | solution.py:40
  107.9 23.2 %all-gather.2 = bf16[1024,256]{1,0:T(8,128)(2,1)S(1)} all-gather(bf16[64,256]{1,0:T(8,128)(2,1)S(1)} %convolution_convert_fusion.5), channel_id=2, replica_groups=mesh['det'=16,'orb'=16] {'orb'}, dimensions={0}, use_global_device_ids=true | all-gather | bytes 557056 | tf_op jit(solution)/shard_map/while/body/eval_jaxpr/all_gather | solution.py:35
  132.5 7.3 %fusion.137 = f32[1024,1,256]{0,2,1:T(8,128)} fusion(bf16[4,256,256]{2,1,0:T(8,128)(2,1)S(1)} %fusion.135, bf16[4,1024,1024]{2,1,0:T(8,128)(2,1)} %get-tuple-element.280, bf16[1024,256]{1,0:T(8,128)(2,1)S(1)} %all-gather.2), kind=kOutput, calls=%fused_computation.12.clone.1 | convolution fusion | flops 2685403136 | bytes 10485760 | tf_op jit(solution)/shard_map/while/body/eval_jaxpr/bqsc,bqdc->sbd/dot_general | solution.py:48
  141.2 2.4 copy.46
  145.5 94.9 %all-reduce.5.cloned.1.call-done = f32[1024,2,256]{2,1,0:T(2,128)} async-done(((f32[1024,2,256]{2,1,0:T(2,128)}), f32[1024,2,256]{2,1,0:T(2,128)}) %all-reduce.5.cloned.1.call-update) | async-done | bytes 2097168 | tf_op jit(solution)/shard_map/while
  242.9 2.3 dynamic_update_slice.17
  246.7 5.5 %collective-permute-done = f32[1,256,256]{2,1,0:T(8,128)S(1)} collective-permute-done((f32[1,256,256]{2,1,0:T(8,128)S(1)}, f32[1,256,256]{2,1,0:T(8,128)S(1)}, u32[]{:S(2)}, u32[]{:S(2)}) %collective-permute-start) | collective-permute-done | bytes 262176 | tf_op jit(solution)/shard_map/while/body/eval_jaxpr/ppermute | solution.py:26
  252.2 2.5 collective-permute-start.1
  254.7 5.5 %collective-permute-done.1 = f32[1,256,256]{2,1,0:T(8,128)S(1)} collective-permute-done((f32[1,256,256]{2,1,0:T(8,128)S(1)}, f32[1,256,256]{2,1,0:T(8,128)S(1)}, u32[]{:S(2)}, u32[]{:S(2)}) %collective-permute-start.1) | collective-permute-done | bytes 262176 | tf_op jit(solution)/shard_map/while/body/eval_jaxpr/ppermute | solution.py:26
  262.3 22.5 %all_gather.19 = bf16[1,1024,256]{2,1,0:T(8,128)(2,1)S(1)} all-gather(bf16[1,64,256]{2,1,0:T(8,128)(2,1)S(1)} %constant_dynamic-slice_fusion.6), channel_id=1, replica_groups=mesh['det'=16,'orb'=16] {'orb'}, dimensions={1}, use_global_device_ids=true | all-gather | bytes 557056 | tf_op jit(solution)/shard_map/while/body/eval_jaxpr/all_gather | solution.py:34
  287.1 5.8 %convolution_convert_fusion.4 = bf16[256,4,1024]{2,0,1:T(8,128)(2,1)S(1)} fusion(bf16[4,1024,1024]{2,1,0:T(8,128)(2,1)} %get-tuple-element.280, bf16[1,1024,256]{2,1,0:T(8,128)(2,1)S(1)} %all_gather.19), kind=kOutput, calls=%fused_computation.10.clone.1 | convolution fusion | flops 2148532224 | bytes 11010048 | tf_op jit(solution)/shard_map/while/body/eval_jaxpr/bsc,qst->bqct/dot_general | solution.py:40
  296.5 22.3 %all-gather.2 = bf16[1024,256]{1,0:T(8,128)(2,1)S(1)} all-gather(bf16[64,256]{1,0:T(8,128)(2,1)S(1)} %convolution_convert_fusion.5), channel_id=2, replica_groups=mesh['det'=16,'orb'=16] {'orb'}, dimensions={0}, use_global_device_ids=true | all-gather | bytes 557056 | tf_op jit(solution)/shard_map/while/body/eval_jaxpr/all_gather | solution.py:35
  320.2 7.3 %fusion.137 = f32[1024,1,256]{0,2,1:T(8,128)} fusion(bf16[4,256,256]{2,1,0:T(8,128)(2,1)S(1)} %fusion.135, bf16[4,1024,1024]{2,1,0:T(8,128)(2,1)} %get-tuple-element.280, bf16[1024,256]{1,0:T(8,128)(2,1)S(1)} %all-gather.2), kind=kOutput, calls=%fused_computation.12.clone.1 | convolution fusion | flops 2685403136 | bytes 10485760 | tf_op jit(solution)/shard_map/while/body/eval_jaxpr/bqsc,bqdc->sbd/dot_general | solution.py:48
  328.9 2.4 copy.46
  333.2 98.3 %all-reduce.5.cloned.1.call-done = f32[1024,2,256]{2,1,0:T(2,128)} async-done(((f32[1024,2,256]{2,1,0:T(2,128)}), f32[1024,2,256]{2,1,0:T(2,128)}) %all-reduce.5.cloned.1.call-update) | async-done | bytes 2097168 | tf_op jit(solution)/shard_map/while
  436.3 2.8 fusion.44
  439.2 4.4 copy.30
  445.0 63.2 %reduce-scatter.2.cloned.1.call-done = f32[4,64,256]{2,1,0:T(8,128)} async-done(((f32[64,64,256]{2,1,0:T(8,128)}), f32[4,64,256]{2,1,0:T(8,128)}) %reduce-scatter.2.cloned.1.call-update) | async-done | bytes 262160 | tf_op jit(solution)/shard_map/reduce_scatter | solution.py:95
  (98 shorter events, 42.1 us)
Async XLA Ops:
  6.5 45.0 %all-gather.5.cloned.1.call-start = ((), (), s32[]{:S(2)}) async-start(), calls=%async_computation.1 | async-start | bytes 2228224 | tf_op jit(solution)/shard_map/all_gather | solution.py:67
  53.8 382.5 %copy-start.4 = (s32[2]{0:T(128)S(1)}, s32[2]{0:T(128)}, u32[]{:S(2)}) copy-start(s32[2]{0:T(128)} %param.12) | copy-start | bytes 28
  53.8 186.6 %all-reduce.5.cloned.1.call-start = ((), (), s32[]{:S(2)}) async-start(), calls=%async_computation.3 | async-start | bytes 4194304 | tf_op jit(solution)/shard_map/while
  54.1 8.5 %collective-permute-start = (f32[1,256,256]{2,1,0:T(8,128)S(1)}, f32[1,256,256]{2,1,0:T(8,128)S(1)}, u32[]{:S(2)}, u32[]{:S(2)}) collective-permute-start(f32[1,256,256]{2,1,0:T(8,128)S(1)} %convolution_bitcast_fusion.4), channel_id=1, source_target_pairs={{0,1},{1,0},{2,3},{3,2},{4,5},{5,4},{6,7},{7,6},{8,9},{9,8},{10,11... | collective-permute-start | bytes 786440 | tf_op jit(solution)/shard_map/while/body/eval_jaxpr/ppermute | solution.py:26
  62.6 9.2 %collective-permute-start.1 = (f32[1,256,256]{2,1,0:T(8,128)S(1)}, f32[1,256,256]{2,1,0:T(8,128)S(1)}, u32[]{:S(2)}, u32[]{:S(2)}) collective-permute-start(f32[1,256,256]{2,1,0:T(8,128)S(1)} %add.115), channel_id=1, source_target_pairs={{0,2},{1,3},{2,0},{3,1},{4,6},{5,7},{6,4},{7,5},{8,10},{9,11},{10,... | collective-permute-start | bytes 786440 | tf_op jit(solution)/shard_map/while/body/eval_jaxpr/ppermute | solution.py:26
  71.8 25.0 %collective-permute-start.2 = (f32[1,256,256]{2,1,0:T(8,128)S(1)}, f32[1,256,256]{2,1,0:T(8,128)S(1)}, u32[]{:S(2)}, u32[]{:S(2)}) collective-permute-start(f32[1,256,256]{2,1,0:T(8,128)S(1)} %add.116), channel_id=1, source_target_pairs={{0,4},{1,5},{2,6},{3,7},{4,0},{5,1},{6,2},{7,3},{8,12},{9,13},{10,... | collective-permute-start | bytes 786440 | tf_op jit(solution)/shard_map/while/body/eval_jaxpr/ppermute | solution.py:26
  96.9 8.6 %collective-permute-start.3 = (f32[1,256,256]{2,1,0:T(8,128)S(1)}, f32[1,256,256]{2,1,0:T(8,128)S(1)}, u32[]{:S(2)}, u32[]{:S(2)}) collective-permute-start(f32[1,256,256]{2,1,0:T(8,128)S(1)} %add.117), channel_id=1, source_target_pairs={{0,8},{1,9},{2,10},{3,11},{4,12},{5,13},{6,14},{7,15},{8,0},{9,1},... | collective-permute-start | bytes 786440 | tf_op jit(solution)/shard_map/while/body/eval_jaxpr/ppermute | solution.py:26
  98.4 7.0 %copy-start.3 = (s32[2,4]{1,0:T(2,128)S(1)}, s32[2,4]{1,0:T(2,128)}, u32[]{:S(2)}) copy-start(s32[2,4]{1,0:T(2,128)} %get-tuple-element.278) | copy-start | bytes 100 | tf_op jit(solution)/shard_map/while
  143.6 0.7 copy-start.5
  143.6 98.4 %copy-start = (f32[2,64,256]{2,0,1:T(2,128)S(1)}, f32[2,64,256]{2,0,1:T(2,128)}, u32[]{:S(2)}) copy-start(f32[2,64,256]{2,0,1:T(2,128)} %get-tuple-element.260) | copy-start | bytes 393220 | tf_op jit(solution)/shard_map/while
  242.9 2.3 copy-start.1
  245.3 186.2 %all-reduce.5.cloned.1.call-start = ((), (), s32[]{:S(2)}) async-start(), calls=%async_computation.3 | async-start | bytes 4194304 | tf_op jit(solution)/shard_map/while
  245.5 6.7 %collective-permute-start = (f32[1,256,256]{2,1,0:T(8,128)S(1)}, f32[1,256,256]{2,1,0:T(8,128)S(1)}, u32[]{:S(2)}, u32[]{:S(2)}) collective-permute-start(f32[1,256,256]{2,1,0:T(8,128)S(1)} %convolution_bitcast_fusion.4), channel_id=1, source_target_pairs={{0,1},{1,0},{2,3},{3,2},{4,5},{5,4},{6,7},{7,6},{8,9},{9,8},{10,11... | collective-permute-start | bytes 786440 | tf_op jit(solution)/shard_map/while/body/eval_jaxpr/ppermute | solution.py:26
  252.2 8.0 %collective-permute-start.1 = (f32[1,256,256]{2,1,0:T(8,128)S(1)}, f32[1,256,256]{2,1,0:T(8,128)S(1)}, u32[]{:S(2)}, u32[]{:S(2)}) collective-permute-start(f32[1,256,256]{2,1,0:T(8,128)S(1)} %add.115), channel_id=1, source_target_pairs={{0,2},{1,3},{2,0},{3,1},{4,6},{5,7},{6,4},{7,5},{8,10},{9,11},{10,... | collective-permute-start | bytes 786440 | tf_op jit(solution)/shard_map/while/body/eval_jaxpr/ppermute | solution.py:26
  260.2 24.6 %collective-permute-start.2 = (f32[1,256,256]{2,1,0:T(8,128)S(1)}, f32[1,256,256]{2,1,0:T(8,128)S(1)}, u32[]{:S(2)}, u32[]{:S(2)}) collective-permute-start(f32[1,256,256]{2,1,0:T(8,128)S(1)} %add.116), channel_id=1, source_target_pairs={{0,4},{1,5},{2,6},{3,7},{4,0},{5,1},{6,2},{7,3},{8,12},{9,13},{10,... | collective-permute-start | bytes 786440 | tf_op jit(solution)/shard_map/while/body/eval_jaxpr/ppermute | solution.py:26
  284.9 9.2 %collective-permute-start.3 = (f32[1,256,256]{2,1,0:T(8,128)S(1)}, f32[1,256,256]{2,1,0:T(8,128)S(1)}, u32[]{:S(2)}, u32[]{:S(2)}) collective-permute-start(f32[1,256,256]{2,1,0:T(8,128)S(1)} %add.117), channel_id=1, source_target_pairs={{0,8},{1,9},{2,10},{3,11},{4,12},{5,13},{6,14},{7,15},{8,0},{9,1},... | collective-permute-start | bytes 786440 | tf_op jit(solution)/shard_map/while/body/eval_jaxpr/ppermute | solution.py:26
  287.1 7.0 %copy-start.3 = (s32[2,4]{1,0:T(2,128)S(1)}, s32[2,4]{1,0:T(2,128)}, u32[]{:S(2)}) copy-start(s32[2,4]{1,0:T(2,128)} %get-tuple-element.278) | copy-start | bytes 100 | tf_op jit(solution)/shard_map/while
  331.3 0.7 copy-start.5
  331.3 101.7 %copy-start = (f32[2,64,256]{2,0,1:T(2,128)S(1)}, f32[2,64,256]{2,0,1:T(2,128)}, u32[]{:S(2)}) copy-start(f32[2,64,256]{2,0,1:T(2,128)} %get-tuple-element.260) | copy-start | bytes 393220 | tf_op jit(solution)/shard_map/while
  434.0 2.3 copy-start.1
  436.3 71.8 %reduce-scatter.2.cloned.1.call-start = ((), (), s32[]{:S(2)}) async-start(), calls=%async_computation.2 | async-start | bytes 4456448 | tf_op jit(solution)/shard_map/reduce_scatter | solution.py:95
  443.6 0.9 copy-start.2
Sparse Core Ops, SparseCore 0:
  9.2 42.3 all-gather.4
  143.8 96.6 all-reduce.4
  331.5 99.9 all-reduce.4
  443.7 64.3 reduce-scatter.1
